TPU v7x, 128 devices: a whole 4x4x4 slice. The times are simulated.
128 devices in a mesh: dp: 32 (over z, y, core), mp: 4 (over x).
Axes of the slice: x: 4, y: 4, z: 4, core: 2. Of those that a mesh axis runs over, the one named last changes fastest.
Arguments:
- tokens: bfloat16 [57344, 1024], P('dp'), may hold values from -60 to 60
- segment_ids: int32 [57344], P('dp'), may hold values from 0 to 127, as said below
- page_table: int32 [448], P('dp'), may hold values from 0 to 447, as said below
- w_query: bfloat16 [1024, 1024], P('dp', 'mp'), may hold values from -0.1875 to 0.1875
- w_key: bfloat16 [1024, 1024], P('dp', 'mp'), may hold values from -0.1875 to 0.1875
- w_value: bfloat16 [1024, 1024], P('dp', 'mp'), may hold values from -0.1875 to 0.1875
- w_out: bfloat16 [1024, 1024], P('mp', 'dp'), may hold values from -1.5 to 1.5
- w_up: bfloat16 [1024, 4096], P('dp', 'mp'), may hold values from -0.1875 to 0.1875
- w_down: bfloat16 [4096, 1024], P('mp', 'dp'), may hold values from -0.09375 to 0.09375
- gain_first: float32 [1024], replicated, may hold values from 0.1 to 1.9
- shift_first: float32 [1024], replicated, may hold values from -3 to 3
- gain_second: float32 [1024], replicated, may hold values from 0.1 to 1.9
- shift_second: float32 [1024], replicated, may hold values from -3 to 3
Outputs:
- mixed: bfloat16 [57344, 1024], P('dp')
- kv_cache: bfloat16 [57344, 2, 1024], P('dp', None, 'mp')
Inputs may be any that keep to these rules, and one draw needn't show every extreme that they name: page_table is a permutation of the page slots. Page p lies on device p // 14 in arrival order and goes to device page_table[p] // 14; from one device at most 1 pages go to one device, and some pair reaches 1. `segment_ids`: tokens with equal ids form one request; after dealing, a request's tokens are consecutive and lie on one device, which holds at most 4 requests.
All inputs are finite; a program needn't handle non-finite values.
Results may differ from a plain program's by a relative error of at most 0.014.
Values may be sent and summed in bfloat16 or wider, within the bound.
No kernel may reach another device: no remote copies, remote signals or barrier semaphores. Data moves between devices by JAX's collectives and lax.ppermute only.
A program may use at most 128 MiB of HBM per device.

v0:
```python
import jax
import jax.numpy as jnp
from jax import lax
from jax.sharding import PartitionSpec as P

HEAD = 64


def layer_norm(hidden_sum, gain, shift):
    center = hidden_sum - jnp.mean(hidden_sum, axis=-1, keepdims=True)
    spread = jnp.mean(center * center, axis=-1, keepdims=True)
    return center * lax.rsqrt(spread + 1e-05) * gain + shift


def attend_head(query, keys, values, segments, block_rows):
    blocks = query.shape[0] // block_rows
    query_blocks = query.reshape(blocks, block_rows, query.shape[1])
    segment_blocks = segments.reshape(blocks, block_rows)

    def per_block(bundle):
        rows, row_ids = bundle
        scores = jnp.einsum("qd,kd->qk", rows, keys, preferred_element_type=jnp.float32) * HEAD ** (
            -0.5
        )
        scores = jnp.where(row_ids[:, None] == segments[None, :], scores, -1e30)
        highest = jnp.max(scores, axis=1, keepdims=True)
        raised = jnp.exp(scores - highest)
        attn_weights = (raised / jnp.sum(raised, axis=1, keepdims=True)).astype(jnp.bfloat16)
        return jnp.dot(attn_weights, values, preferred_element_type=jnp.float32).astype(
            jnp.bfloat16
        )

    return lax.map(per_block, (query_blocks, segment_blocks)).reshape(
        query.shape[0], values.shape[1]
    )


def finish(partial_value, residual, gain, shift):
    total = lax.psum(partial_value.astype(jnp.bfloat16), "mp").astype(jnp.float32)
    return layer_norm(residual.astype(jnp.float32) + total, gain, shift).astype(jnp.bfloat16)


def outgoing_pages(source, got_slots, pages_dev, page):
    paged = source.reshape(pages_dev, page, source.shape[1])[jnp.clip(got_slots, 0, pages_dev - 1)]
    return jnp.where((got_slots >= 0)[:, None, None], paged, jnp.zeros_like(paged))


def body(
    tokens,
    segment_ids,
    page_table,
    w_query,
    w_key,
    w_value,
    w_out,
    w_up,
    w_down,
    gain_first,
    shift_first,
    gain_second,
    shift_second,
):
    n_data = lax.axis_size("dp")
    pages_dev = page_table.shape[0]
    page = tokens.shape[0] // pages_dev
    width = tokens.shape[1]
    slots_per = (pages_dev + n_data - 1) // n_data
    buffer_rows = n_data * slots_per
    target = page_table // pages_dev
    local_slot = page_table % pages_dev
    order = jnp.arange(pages_dev, dtype=jnp.int32)
    earlier = (target[:, None] == target[None, :]) & (order[:, None] < order[None, :])
    rank = jnp.sum(earlier.astype(jnp.int32), axis=0)
    position = target * slots_per + rank
    send_ids = (
        jnp.zeros((buffer_rows, page), jnp.int32)
        .at[position]
        .set(segment_ids.reshape(pages_dev, page))
    )
    send_slots = jnp.full((buffer_rows,), -1, jnp.int32).at[position].set(local_slot)
    send_pages = (
        jnp.zeros((buffer_rows, page, width), tokens.dtype)
        .at[position]
        .set(tokens.reshape(pages_dev, page, width))
    )
    got_pages, got_ids, got_slots = (
        lax.all_to_all(send_pages, "dp", split_axis=0, concat_axis=0, tiled=True),
        lax.all_to_all(send_ids, "dp", split_axis=0, concat_axis=0, tiled=True),
        lax.all_to_all(send_slots, "dp", split_axis=0, concat_axis=0, tiled=True),
    )
    matches = got_slots[None, :] == order[:, None]
    source_row = jnp.sum(
        jnp.where(matches, jnp.arange(buffer_rows, dtype=jnp.int32)[None, :], 0), axis=1
    )
    dealt = got_pages[source_row].reshape(pages_dev * page, got_pages.shape[2])
    dealt_ids = got_ids[source_row].reshape(pages_dev * page)
    full_query, full_key, full_value, full_up, full_out, full_down = (
        lax.all_gather(w_query, "dp", axis=0, tiled=True),
        lax.all_gather(w_key, "dp", axis=0, tiled=True),
        lax.all_gather(w_value, "dp", axis=0, tiled=True),
        lax.all_gather(w_up, "dp", axis=0, tiled=True),
        lax.all_gather(w_out, "dp", axis=1, tiled=True),
        lax.all_gather(w_down, "dp", axis=1, tiled=True),
    )
    query = jnp.dot(dealt, full_query, preferred_element_type=jnp.float32).astype(jnp.bfloat16)
    keys = jnp.dot(dealt, full_key, preferred_element_type=jnp.float32).astype(jnp.bfloat16)
    values = jnp.dot(dealt, full_value, preferred_element_type=jnp.float32).astype(jnp.bfloat16)
    suitable = [
        count for count in range(1, pages_dev + 1) if pages_dev % count == 0 and count * page >= 512
    ]
    block_rows = suitable[0] * page
    heads_here = query.shape[1] // HEAD
    contexts = []
    for head in range(heads_here):
        cols = slice(head * HEAD, (head + 1) * HEAD)
        contexts.append(
            attend_head(query[:, cols], keys[:, cols], values[:, cols], dealt_ids, block_rows)
        )
    context = jnp.concatenate(contexts, axis=1)
    partial_value = jnp.dot(context, full_out, preferred_element_type=jnp.float32)
    first = finish(partial_value, dealt, gain_first, shift_first)
    hidden = jax.nn.gelu(
        jnp.dot(first, full_up, preferred_element_type=jnp.float32), approximate=False
    ).astype(jnp.bfloat16)
    second = finish(
        jnp.dot(hidden, full_down, preferred_element_type=jnp.float32),
        first,
        gain_second,
        shift_second,
    )
    returned = lax.all_to_all(
        outgoing_pages(second, got_slots, pages_dev, page),
        "dp",
        split_axis=0,
        concat_axis=0,
        tiled=True,
    )
    mixed = returned[position].reshape(pages_dev * page, width)
    kv_cache = jnp.stack([keys, values], axis=1)
    return (mixed, kv_cache)


def solution(mesh):
    return jax.shard_map(
        body,
        mesh=mesh,
        in_specs=(
            P("dp", None),
            P("dp"),
            P("dp"),
            P("dp", "mp"),
            P("dp", "mp"),
            P("dp", "mp"),
            P("mp", "dp"),
            P("dp", "mp"),
            P("mp", "dp"),
            P(),
            P(),
            P(),
            P(),
        ),
        out_specs=(P("dp", None), P("dp", None, "mp")),
        check_vma=False,
    )
```

profile of v0, /device:TPU:0, one launch (start us, length us, event | category | flops | bytes accessed | tf_op | source)
XLA Modules:
  0.0 663.7 jit_solution(7760421901178392480)
XLA Ops:
  10.1 8.4 %all-to-all-start = ((s32[32,1,1]{2,1,0:T(1,128)}), s32[32,1,1]{2,1,0:T(1,128)S(1)}, u32[]{:S(2)}, u32[]{:S(2)}) async-start(s32[32,1,1]{2,1,0:T(1,128)} %copy.81), calls=%async_computation | async-start | bytes 32768 | tf_op jit(solution)/shard_map/all_to_all | solution.py:89
  19.8 6.1 all-to-all-done
  25.9 3.8 all-to-all-start.2
  29.7 4.3 broadcast.142
  34.0 10.6 %scatter_fusion = bf16[32,128,1024]{2,1,0:T(8,128)(2,1)} fusion(bf16[32,128,1024]{2,1,0:T(8,128)(2,1)} %broadcast.142, s32[14]{0:T(128)S(1)} %compare_select_fusion.2, bf16[14,128,1024]{2,1,0:T(8,128)(2,1)} %bitcast.139), kind=kCustom, calls=%fused_computation.5 | custom fusion | bytes 11010104 | tf_op jit(solution)/shard_map/scatter | solution.py:84
  44.6 7.7 %all-to-all-start.1 = ((bf16[32,128,1024]{2,1,0:T(8,128)(2,1)}), bf16[32,128,1024]{2,1,0:T(8,128)(2,1)}, u32[]{:S(2)}, u32[]{:S(2)}) async-start(bf16[32,128,1024]{2,1,0:T(8,128)(2,1)} %scatter_fusion), calls=%async_computation.1 | async-start | bytes 16777216 | tf_op jit(solution)/shard_map/all_to_all | solution.py:87
  52.4 119.4 %all_gather.19 = bf16[1024,256]{1,0:T(8,128)(2,1)S(1)} all-gather(bf16[32,256]{1,0:T(8,128)(2,1)S(1)} %copy-done.16), channel_id=1, replica_groups=mesh['dp'=32,'mp'=4] {'dp'}, dimensions={0}, use_global_device_ids=true | all-gather | bytes 540672 | tf_op jit(solution)/shard_map/all_gather | solution.py:99
  171.8 25.5 %all_gather.20 = bf16[1024,256]{1,0:T(8,128)(2,1)S(1)} all-gather(bf16[32,256]{1,0:T(8,128)(2,1)S(1)} %copy-done.17), channel_id=1, replica_groups=mesh['dp'=32,'mp'=4] {'dp'}, dimensions={0}, use_global_device_ids=true | all-gather | bytes 540672 | tf_op jit(solution)/shard_map/all_gather | solution.py:100
  197.2 22.1 %all_gather.18 = bf16[1024,256]{1,0:T(8,128)(2,1)S(1)} all-gather(bf16[32,256]{1,0:T(8,128)(2,1)S(1)} %copy-done.18), channel_id=1, replica_groups=mesh['dp'=32,'mp'=4] {'dp'}, dimensions={0}, use_global_device_ids=true | all-gather | bytes 540672 | tf_op jit(solution)/shard_map/all_gather | solution.py:98
  219.3 27.3 %all_gather.21 = bf16[256,1024]{0,1:T(8,128)(2,1)} all-gather(bf16[256,32]{0,1:T(8,128)(2,1)S(1)} %copy-done.19), channel_id=1, replica_groups=mesh['dp'=32,'mp'=4] {'dp'}, dimensions={1}, use_global_device_ids=true | all-gather | bytes 540672 | tf_op jit(solution)/shard_map/all_gather | solution.py:102
  246.7 1.6 clamp_reduce_fusion
  249.0 6.1 gather_fusion
  255.1 3.2 convolution_convert_fusion.3
  260.3 3.2 convolution_convert_fusion.2
  265.4 3.2 convolution_convert_fusion.4
  269.7 7.8 %while.40 = (s32[]{:T(128)}, bf16[2,896,64]{1,2,0:T(8,128)(2,1)S(1)}, s32[2,896]{1,0:T(2,128)S(1)}, s32[14,128]{1,0:T(8,128)S(1)}, bf16[2,896,64]{2,1,0:T(8,128)...) while((s32[]{:T(128)}, bf16[2,896,64]{1,2,0:T(8,128)(2,1)S(1)}, ...), condition=%wide.region_8.9_spmd, body=%wide.region_5.8_spmd.sunk | while | flops 425548032 | bytes 20567648 | solution.py:33
  272.2 1.5 fusion.144
  276.0 1.5 fusion.144
  279.1 7.7 %while.41 = (s32[]{:T(128)}, bf16[2,896,64]{1,2,0:T(8,128)(2,1)S(1)}, s32[2,896]{1,0:T(2,128)S(1)}, s32[14,128]{1,0:T(8,128)S(1)}, bf16[2,896,64]{2,1,0:T(8,128)...) while((s32[]{:T(128)}, bf16[2,896,64]{1,2,0:T(8,128)(2,1)S(1)}, ...), condition=%wide.region_12.13_spmd, body=%wide.region_9.12_spmd.sunk | while | flops 425548032 | bytes 20567648 | solution.py:33
  279.2 1.2 fusion.147
  281.4 1.5 fusion.149
  283.0 1.2 fusion.147
  285.2 1.5 fusion.149
  287.7 7.7 %while.42 = (s32[]{:T(128)}, bf16[2,896,64]{1,2,0:T(8,128)(2,1)S(1)}, s32[2,896]{1,0:T(2,128)S(1)}, s32[14,128]{1,0:T(8,128)S(1)}, bf16[2,896,64]{2,1,0:T(8,128)...) while((s32[]{:T(128)}, bf16[2,896,64]{1,2,0:T(8,128)(2,1)S(1)}, ...), condition=%wide.region_16.17_spmd, body=%wide.region_13.16_spmd.sunk | while | flops 425548032 | bytes 20567648 | solution.py:33
  287.7 1.2 fusion.152
  290.0 1.5 fusion.154
  291.6 1.2 fusion.152
  293.8 1.5 fusion.154
  296.3 7.9 %while.43 = (s32[]{:T(128)}, bf16[2,896,64]{1,2,0:T(8,128)(2,1)S(1)}, s32[2,896]{1,0:T(2,128)S(1)}, s32[14,128]{1,0:T(8,128)S(1)}, bf16[2,896,64]{2,1,0:T(8,128)...) while((s32[]{:T(128)}, bf16[2,896,64]{1,2,0:T(8,128)(2,1)S(1)}, ...), condition=%wide.region_20.21_spmd, body=%wide.region_17.20_spmd.sunk | while | flops 425548032 | bytes 20567648 | solution.py:33
  298.8 1.5 fusion.159
  302.6 1.5 fusion.159
  304.2 3.0 convolution_convert_fusion
  308.5 81.5 %all-reduce.3.cloned.1.call-done = bf16[1792,1024]{1,0:T(8,128)(2,1)} async-done(((bf16[1792,1024]{1,0:T(8,128)(2,1)}), bf16[1792,1024]{1,0:T(8,128)(2,1)}) %all-reduce.3.cloned.1.call-update) | async-done | bytes 3670032 | tf_op jit(solution)/shard_map/psum | solution.py:39
  390.0 4.3 fusion.43
  395.5 2.3 multiply_reduce_fusion.1
  397.8 3.3 add_convert_fusion.1
  401.1 26.1 %convolution_convert_fusion.1 = bf16[1792,1024]{1,0:T(8,128)(2,1)} fusion(bf16[1024,1024]{0,1:T(8,128)(2,1)} %all-gather.5.cloned.1.call-done, bf16[1792,1024]{1,0:T(8,128)(2,1)} %add_convert_fusion.1, bf16[1024,1024]{1,0:T(8,128)(2,1)} %all-gather.3.cloned.1.call-done), kind=kOutput, calls=%fused_computation.86 | convolution fusion | flops 7637303296 | bytes 11534336 | tf_op jit(solution)/shard_map/dot_general | solution.py:126
  428.0 83.4 %all-reduce.5.cloned.1.call-done = bf16[1792,1024]{1,0:T(8,128)(2,1)} async-done(((bf16[1792,1024]{1,0:T(8,128)(2,1)}), bf16[1792,1024]{1,0:T(8,128)(2,1)}) %all-reduce.5.cloned.1.call-update) | async-done | bytes 3670032 | tf_op jit(solution)/shard_map/psum | solution.py:39
  511.4 4.3 fusion.45
  516.7 2.4 multiply_reduce_fusion
  519.2 3.3 add_convert_fusion
  522.5 6.9 %gather_fusion.2 = bf16[32,128,1024]{2,1,0:T(8,128)(2,1)} fusion(bf16[14,128,1024]{2,1,0:T(8,128)(2,1)} %bitcast.136, s32[1024]{0:T(1024)S(1)} %pad_clamp_fusion.1), kind=kCustom, calls=%fused_computation.2 | custom fusion | bytes 16777344 | tf_op jit(solution)/shard_map/gather | solution.py:44
  529.5 7.2 %broadcast_select_fusion = bf16[32,128,1024]{2,1,0:T(8,128)(2,1)} fusion(bf16[32,128,1024]{2,1,0:T(8,128)(2,1)} %gather_fusion.2, pred[32]{0:T(512)(128)(4,1)S(1)} %compare_reduce_fusion), kind=kLoop, calls=%fused_computation.56 | loop fusion | flops 4194304 | bytes 16777248 | tf_op jit(solution)/shard_map/jit(_where)/select_n | solution.py:45
  536.7 7.5 %all-to-all-start.3 = ((bf16[32,128,1024]{2,1,0:T(8,128)(2,1)}), bf16[32,128,1024]{2,1,0:T(8,128)(2,1)}, u32[]{:S(2)}, u32[]{:S(2)}) async-start(bf16[32,128,1024]{2,1,0:T(8,128)(2,1)} %broadcast_select_fusion), calls=%async_computation.3 | async-start | bytes 16777216 | tf_op jit(solution)/shard_map/all_to_all | solution.py:131
  544.3 1.4 pad_maximum_fusion
  545.6 3.6 copy.98
  549.2 100.9 %all-to-all-done.3 = bf16[32,128,1024]{2,1,0:T(8,128)(2,1)} async-done(((bf16[32,128,1024]{2,1,0:T(8,128)(2,1)}), bf16[32,128,1024]{2,1,0:T(8,128)(2,1)}, u32[]{:S(2)}, u32[]{:S(2)}) %all-to-all-start.3) | async-done | bytes 8388640 | tf_op jit(solution)/shard_map/all_to_all | solution.py:131
  650.1 6.0 gather_fusion.3
  (128 shorter events, 29.7 us)
Async XLA Ops:
  8.0 10.6 %copy-start = (s32[1792]{0:T(1024)S(1)}, s32[1792]{0:T(1024)}, u32[]{:S(2)}) copy-start(s32[1792]{0:T(1024)} %param.22) | copy-start | bytes 21508
  8.8 35.8 %copy-start.24 = (s32[14]{0:T(128)}, s32[14]{0:T(128)S(1)}, u32[]{:S(2)}) copy-start(s32[14]{0:T(128)S(1)} %compare_select_fusion.2) | copy-start | bytes 172
  10.1 15.8 %all-to-all-start = ((s32[32,1,1]{2,1,0:T(1,128)}), s32[32,1,1]{2,1,0:T(1,128)S(1)}, u32[]{:S(2)}, u32[]{:S(2)}) async-start(s32[32,1,1]{2,1,0:T(1,128)} %copy.81), calls=%async_computation | async-start | bytes 32768 | tf_op jit(solution)/shard_map/all_to_all | solution.py:89
  25.9 220.8 %copy-start.14 = (s32[32,1,1]{2,1,0:T(1,128)}, s32[32,1,1]{2,1,0:T(1,128)S(1)}, u32[]{:S(2)}) copy-start(s32[32,1,1]{2,1,0:T(1,128)S(1)} %all-to-all-done) | copy-start | bytes 388
  25.9 18.8 %all-to-all-start.2 = ((s32[32,1,128]{2,1,0:T(1,128)}), s32[32,1,128]{2,1,0:T(1,128)S(1)}, u32[]{:S(2)}, u32[]{:S(2)}) async-start(s32[32,1,128]{2,1,0:T(1,128)} %bitcast.18), calls=%async_computation.2 | async-start | bytes 32768 | tf_op jit(solution)/shard_map/all_to_all | solution.py:88
  44.6 7.8 %copy-start.16 = (bf16[32,256]{1,0:T(8,128)(2,1)S(1)}, bf16[32,256]{1,0:T(8,128)(2,1)}, u32[]{:S(2)}) copy-start(bf16[32,256]{1,0:T(8,128)(2,1)} %param.25) | copy-start | bytes 49156
  44.6 127.1 %copy-start.17 = (bf16[32,256]{1,0:T(8,128)(2,1)S(1)}, bf16[32,256]{1,0:T(8,128)(2,1)}, u32[]{:S(2)}) copy-start(bf16[32,256]{1,0:T(8,128)(2,1)} %param.26) | copy-start | bytes 49156
  44.6 152.6 %copy-start.18 = (bf16[32,256]{1,0:T(8,128)(2,1)S(1)}, bf16[32,256]{1,0:T(8,128)(2,1)}, u32[]{:S(2)}) copy-start(bf16[32,256]{1,0:T(8,128)(2,1)} %param.24) | copy-start | bytes 49156
  44.6 174.7 %copy-start.19 = (bf16[256,32]{0,1:T(8,128)(2,1)S(1)}, bf16[256,32]{0,1:T(8,128)(2,1)}, u32[]{:S(2)}) copy-start(bf16[256,32]{0,1:T(8,128)(2,1)} %param.27) | copy-start | bytes 49156
  44.6 204.4 %all-to-all-start.1 = ((bf16[32,128,1024]{2,1,0:T(8,128)(2,1)}), bf16[32,128,1024]{2,1,0:T(8,128)(2,1)}, u32[]{:S(2)}, u32[]{:S(2)}) async-start(bf16[32,128,1024]{2,1,0:T(8,128)(2,1)} %scatter_fusion), calls=%async_computation.1 | async-start | bytes 16777216 | tf_op jit(solution)/shard_map/all_to_all | solution.py:87
  52.3 337.7 %all-reduce.3.cloned.1.call-start = ((), (), s32[]{:S(2)}) async-start(), calls=%async_computation.4 | async-start | bytes 7340032 | tf_op jit(solution)/shard_map/psum | solution.py:39
  258.3 0.9 copy-start.6
  263.5 0.9 copy-start.8
  287.7 7.7 %copy-start.9 = (bf16[1792,64]{0,1:T(8,128)(2,1)S(1)}, bf16[1792,64]{0,1:T(8,128)(2,1)}, u32[]{:S(2)}) copy-start(bf16[1792,64]{0,1:T(8,128)(2,1)} %get-tuple-element.375) | copy-start | bytes 688132
  287.7 8.0 %copy-start.10 = (bf16[1792,64]{0,1:T(8,128)(2,1)S(1)}, bf16[1792,64]{0,1:T(8,128)(2,1)}, u32[]{:S(2)}) copy-start(bf16[1792,64]{0,1:T(8,128)(2,1)} %get-tuple-element.371) | copy-start | bytes 688132
  287.7 8.3 %copy-start.11 = (bf16[1792,64]{0,1:T(8,128)(2,1)S(1)}, bf16[1792,64]{0,1:T(8,128)(2,1)}, u32[]{:S(2)}) copy-start(bf16[1792,64]{0,1:T(8,128)(2,1)} %get-tuple-element.379) | copy-start | bytes 688132
  296.3 7.9 %copy-start.12 = (bf16[256,1024]{0,1:T(8,128)(2,1)S(1)}, bf16[256,1024]{0,1:T(8,128)(2,1)}, u32[]{:S(2)}) copy-start(bf16[256,1024]{0,1:T(8,128)(2,1)} %all_gather.21) | copy-start | bytes 1572868
  296.3 7.9 %copy-start.13 = (bf16[2,8,8,896]{3,2,0,1:T(8,128)(2,1)S(1)}, bf16[2,8,8,896]{3,2,0,1:T(8,128)(2,1)}, u32[]{:S(2)}) copy-start(bf16[2,8,8,896]{3,2,0,1:T(8,128)(2,1)} %copy.103) | copy-start | bytes 688132
  307.3 93.9 %all-gather.3.cloned.1.call-start = ((), (), s32[]{:S(2)}) async-start(), calls=%async_computation.5 | async-start | bytes 2162688 | tf_op jit(solution)/shard_map/all_gather | solution.py:101
  307.8 93.3 %all-gather.5.cloned.1.call-start = ((), (), s32[]{:S(2)}) async-start(), calls=%async_computation.6 | async-start | bytes 2162688 | tf_op jit(solution)/shard_map/all_gather | solution.py:103
  308.4 89.3 %copy-start.20 = (f32[1024]{0:T(1024)S(1)}, f32[1024]{0:T(1024)}, u32[]{:S(2)}) copy-start(f32[1024]{0:T(1024)} %param.31) | copy-start | bytes 12292
  308.4 89.3 %copy-start.21 = (f32[1024]{0:T(1024)S(1)}, f32[1024]{0:T(1024)}, u32[]{:S(2)}) copy-start(f32[1024]{0:T(1024)} %param.30) | copy-start | bytes 12292
  308.5 203.0 %all-reduce.5.cloned.1.call-start = ((), (), s32[]{:S(2)}) async-start(), calls=%async_computation.7 | async-start | bytes 7340032 | tf_op jit(solution)/shard_map/psum | solution.py:39
  390.0 4.4 copy-start.2
  390.0 5.5 copy-start.4
  401.1 26.1 %copy-start.26 = (s32[32]{0:T(128)S(1)}, s32[32]{0:T(128)}, u32[]{:S(2)}) copy-start(s32[32]{0:T(128)} %get-tuple-element.304) | copy-start | bytes 388
  401.1 26.2 %copy-start.15 = (s32[32,1,1]{2,1,0:T(1,128)S(1)}, s32[32,1,1]{2,1,0:T(1,128)}, u32[]{:S(2)}) copy-start(s32[32,1,1]{2,1,0:T(1,128)} %copy-done.14) | copy-start | bytes 388
  428.0 91.2 %copy-start.22 = (f32[1024]{0:T(1024)S(1)}, f32[1024]{0:T(1024)}, u32[]{:S(2)}) copy-start(f32[1024]{0:T(1024)} %param.33) | copy-start | bytes 12292
  428.0 91.2 %copy-start.23 = (f32[1024]{0:T(1024)S(1)}, f32[1024]{0:T(1024)}, u32[]{:S(2)}) copy-start(f32[1024]{0:T(1024)} %param.32) | copy-start | bytes 12292
  511.4 4.3 copy-start.3
  511.4 5.3 copy-start.5
  536.7 7.5 %copy-start.25 = (s32[14]{0:T(128)S(1)}, s32[14]{0:T(128)}, u32[]{:S(2)}) copy-start(s32[14]{0:T(128)} %copy-done.24) | copy-start | bytes 172
  536.7 7.6 %copy-start.7 = (bf16[1792,256]{0,1:T(8,128)(2,1)S(1)}, bf16[1792,256]{0,1:T(8,128)(2,1)}, u32[]{:S(2)}) copy-start(bf16[1792,256]{0,1:T(8,128)(2,1)} %copy-done.6) | copy-start | bytes 2752516
  536.7 113.4 %all-to-all-start.3 = ((bf16[32,128,1024]{2,1,0:T(8,128)(2,1)}), bf16[32,128,1024]{2,1,0:T(8,128)(2,1)}, u32[]{:S(2)}, u32[]{:S(2)}) async-start(bf16[32,128,1024]{2,1,0:T(8,128)(2,1)} %broadcast_select_fusion), calls=%async_computation.3 | async-start | bytes 16777216 | tf_op jit(solution)/shard_map/all_to_all | solution.py:131
  544.3 111.9 %copy-start.1 = (s32[1792]{0:T(1024)S(1)}, s32[1792]{0:T(1024)}, u32[]{:S(2)}) copy-start(s32[1792]{0:T(1024)} %param.22) | copy-start | bytes 21508
Sparse Core Ops, SparseCore 0:
  307.4 82.5 all-reduce.2
  427.4 84.0 all-reduce.4
Sparse Core Ops, SparseCore 1:
  310.0 42.0 all-gather.2
  354.2 42.9 all-gather.4
where the time goes:
time: 670 us; the launch traced here: 664 us
  waiting for transfers between devices  273 us (41%)
  blocking collectives  194 us (29%)
  matrix products  60.8 us (9%)
  local copies, waits for them, and re-layouts  51.1 us (8%)
  other arithmetic  40.1 us (6%)
  starting transfers between devices  27.6 us (4%)
  between operations  16.2 us (2%)
    psum x2, waiting for transfers between devices, finish(): lax.psum(partial_value.astype(jnp.bfloat16), 'mp').astype(jnp.float32)  165 us
    all_gather x1, blocking collectives, body(): lax.all_gather(w_key, 'dp', axis=0, tiled=True)  119 us
    all_to_all x1, waiting for transfers between devices, body(): lax.all_to_all(outgoing_pages(second, got_slots, pages_dev, page), 'dp',...  101 us
    all_gather x1, blocking collectives, body(): lax.all_gather(w_out, 'dp', axis=1, tiled=True)  27.3 us
    dot_general x1, matrix products, body(): jnp.dot(hidden, full_down, preferred_element_type=jnp.float32)  26.1 us
    all_gather x1, blocking collectives, body(): lax.all_gather(w_value, 'dp', axis=0, tiled=True)  25.5 us
    all_gather x1, blocking collectives, body(): lax.all_gather(w_query, 'dp', axis=0, tiled=True)  22.1 us
  transfers between devices with their start and end apart: 8, of which 4 were waited for; matrix products, arithmetic and copies ran while one was open for 5% of the time, Pallas kernels for 0%

commit v1 on v0

--- a/solution.py
+++ b/solution.py
@@ -36,7 +36,9 @@
 
 
 def finish(partial_value, residual, gain, shift):
-    total = lax.psum(partial_value.astype(jnp.bfloat16), "mp").astype(jnp.float32)
+    total = jnp.sum(lax.all_gather(partial_value.astype(jnp.bfloat16), "mp"), axis=0).astype(
+        jnp.float32
+    )
     return layer_norm(residual.astype(jnp.float32) + total, gain, shift).astype(jnp.bfloat16)
 
 

time: 670 us -> 871 us (1.30)
  waiting for transfers between devices: 273 us -> 447 us
  other arithmetic: 40.1 us -> 70.1 us
    all_gather x0 -> x2, waiting for transfers between devices: none -> 268 us  [finish(): lax.all_gather(partial_value.astype(jnp.bfloat16), 'mp')]
    psum x2 -> x0, waiting for transfers between devices: 165 us -> none  [finish(): lax.psum(partial_value.astype(jnp.bfloat16), 'mp').astype(jnp.float32)]
    all_gather x1, blocking collectives: 22.1 us -> 119 us  [body(): lax.all_gather(w_query, 'dp', axis=0, tiled=True)]
    all_gather x1, blocking collectives: 119 us -> 25.5 us  [body(): lax.all_gather(w_key, 'dp', axis=0, tiled=True)]
    all_gather x1, waiting for transfers between devices: 0.01 us -> 45.3 us  [body(): lax.all_gather(w_down, 'dp', axis=1, tiled=True)]
    all_gather x1, waiting for transfers between devices: 0.01 us -> 24.9 us  [body(): lax.all_gather(w_up, 'dp', axis=0, tiled=True)]
    reduce_sum x0 -> x2, other arithmetic: none -> 22.3 us  [finish(): jnp.sum(lax.all_gather(partial_value.astype(jnp.bfloat16), 'mp'), axis=0)]
  transfers between devices with their start and end apart: 8 -> 8, of which waited for: 4 -> 6; matrix products, arithmetic and copies ran while one was open for 5% -> 5% of each run, Pallas kernels for 0% -> 0%
where the time goes in v1:
time: 871 us; the launch traced here: 864 us
  waiting for transfers between devices  447 us (51%)
  blocking collectives  194 us (22%)
  other arithmetic  70.1 us (8%)
  matrix products  59.2 us (7%)
  local copies, waits for them, and re-layouts  51.1 us (6%)
  starting transfers between devices  27.6 us (3%)
  between operations  14.5 us (2%)
    all_gather x2, waiting for transfers between devices, finish(): lax.all_gather(partial_value.astype(jnp.bfloat16), 'mp')  268 us
    all_gather x1, blocking collectives, body(): lax.all_gather(w_query, 'dp', axis=0, tiled=True)  119 us
    all_to_all x1, waiting for transfers between devices, body(): lax.all_to_all(outgoing_pages(second, got_slots, pages_dev, page), 'dp',...  101 us
    all_gather x1, waiting for transfers between devices, body(): lax.all_gather(w_down, 'dp', axis=1, tiled=True)  45.3 us
    all_gather x1, blocking collectives, body(): lax.all_gather(w_out, 'dp', axis=1, tiled=True)  27.3 us
    dot_general x1, matrix products, body(): jnp.dot(hidden, full_down, preferred_element_type=jnp.float32)  26.1 us
    all_gather x1, blocking collectives, body(): lax.all_gather(w_key, 'dp', axis=0, tiled=True)  25.5 us
    all_gather x1, waiting for transfers between devices, body(): lax.all_gather(w_up, 'dp', axis=0, tiled=True)  24.9 us
  transfers between devices with their start and end apart: 8, of which 6 were waited for; matrix products, arithmetic and copies ran while one was open for 5% of the time, Pallas kernels for 0%

profile of v1, /device:TPU:0, one launch (start us, length us, event | category | flops | bytes accessed | tf_op | source)
XLA Modules:
  0.0 864.2 jit_solution(7369539744846020982)
XLA Ops:
  9.3 8.4 all-to-all-start
  18.9 6.1 all-to-all-done
  25.0 3.8 all-to-all-start.2
  28.9 4.3 broadcast.272
  33.2 10.6 %scatter_fusion = bf16[32,128,1024]{2,1,0:T(8,128)(2,1)} fusion(bf16[32,128,1024]{2,1,0:T(8,128)(2,1)} %broadcast.272, s32[14]{0:T(128)S(1)} %compare_select_fusion.2, bf16[14,128,1024]{2,1,0:T(8,128)(2,1)} %bitcast.158), kind=kCustom, calls=%fused_computation.5 | custom fusion | bytes 11010104 | tf_op jit(solution)/shard_map/scatter | solution.py:86
  43.8 7.7 all-to-all-start.1
  51.5 119.4 %all_gather.30 = bf16[1024,256]{1,0:T(8,128)(2,1)S(1)} all-gather(bf16[32,256]{1,0:T(8,128)(2,1)S(1)} %copy-done.22), channel_id=1, replica_groups=mesh['dp'=32,'mp'=4] {'dp'}, dimensions={0}, use_global_device_ids=true | all-gather | bytes 540672 | tf_op jit(solution)/shard_map/all_gather | solution.py:100
  170.9 25.5 %all_gather.31 = bf16[1024,256]{1,0:T(8,128)(2,1)S(1)} all-gather(bf16[32,256]{1,0:T(8,128)(2,1)S(1)} %copy-done.23), channel_id=1, replica_groups=mesh['dp'=32,'mp'=4] {'dp'}, dimensions={0}, use_global_device_ids=true | all-gather | bytes 540672 | tf_op jit(solution)/shard_map/all_gather | solution.py:101
  196.4 22.1 %all_gather.32 = bf16[1024,256]{1,0:T(8,128)(2,1)S(1)} all-gather(bf16[32,256]{1,0:T(8,128)(2,1)S(1)} %copy-done.24), channel_id=1, replica_groups=mesh['dp'=32,'mp'=4] {'dp'}, dimensions={0}, use_global_device_ids=true | all-gather | bytes 540672 | tf_op jit(solution)/shard_map/all_gather | solution.py:102
  218.5 27.3 %all_gather.33 = bf16[256,1024]{0,1:T(8,128)(2,1)} all-gather(bf16[256,32]{0,1:T(8,128)(2,1)S(1)} %copy-done.25), channel_id=1, replica_groups=mesh['dp'=32,'mp'=4] {'dp'}, dimensions={1}, use_global_device_ids=true | all-gather | bytes 540672 | tf_op jit(solution)/shard_map/all_gather | solution.py:104
  245.8 1.6 clamp_reduce_fusion
  248.2 6.1 gather_fusion
  254.2 3.4 convolution_convert_fusion.2
  267.8 10.2 %while.40 = (s32[]{:T(128)}, bf16[2,896,64]{1,2,0:T(8,128)(2,1)S(1)}, s32[2,896]{1,0:T(2,128)S(1)}, s32[14,128]{1,0:T(8,128)S(1)}, bf16[2,896,64]{2,1,0:T(8,128)...) while((s32[]{:T(128)}, bf16[2,896,64]{1,2,0:T(8,128)(2,1)S(1)}, ...), condition=%wide.region_8.9_spmd, body=%wide.region_5.8_spmd.sunk | while | flops 425548032 | bytes 20566120 | solution.py:33
  268.0 2.4 fusion.143
  271.4 1.5 fusion.145
  273.0 2.4 fusion.143
  276.4 1.5 fusion.145
  278.9 7.7 while.43
  281.2 1.5 fusion.160
  285.1 1.5 fusion.160
  287.0 7.7 while.42
  289.3 1.5 fusion.155
  293.1 1.5 fusion.155
  295.0 7.9 while.41
  297.5 1.5 fusion.150
  301.4 1.5 fusion.150
  303.0 3.0 convolution_convert_fusion
  307.5 133.3 %all-gather.11.cloned.1.call-done = bf16[7168,1024]{1,0:T(8,128)(2,1)} async-done(((bf16[1792,1024]{1,0:T(8,128)(2,1)}), bf16[7168,1024]{1,0:T(8,128)(2,1)}) %all-gather.11.cloned.1.call-update) | async-done | bytes 14680080 | tf_op jit(solution)/shard_map/all_gather | solution.py:39
  440.8 11.0 %reduce_sum.119 = bf16[1792,1024]{1,0:T(8,128)(2,1)} reduce(bf16[4,1792,1024]{2,1,0:T(8,128)(2,1)} %bitcast.154, bf16[]{:T(256)} %constant.100.clone.1), dimensions={0}, to_apply=%region_21.22 | reduce | flops 5505024 | bytes 18350082 | tf_op jit(solution)/shard_map/reduce_sum | solution.py:39
  451.8 4.4 fusion.44
  457.2 2.3 multiply_reduce_fusion.1
  459.5 3.4 add_convert_fusion.1
  462.9 24.9 %all-gather.7.cloned.1.call-done = bf16[1024,1024]{1,0:T(8,128)(2,1)} async-done(((bf16[32,1024]{1,0:T(8,128)(2,1)}), bf16[1024,1024]{1,0:T(8,128)(2,1)}) %all-gather.7.cloned.1.call-update) | async-done | bytes 2097168 | tf_op jit(solution)/shard_map/all_gather | solution.py:103
  487.8 45.3 %all-gather.9.cloned.1.call-done = bf16[1024,1024]{0,1:T(8,128)(2,1)} async-done(((bf16[1024,32]{0,1:T(8,128)(2,1)}), bf16[1024,1024]{0,1:T(8,128)(2,1)}) %all-gather.9.cloned.1.call-update) | async-done | bytes 2097168 | tf_op jit(solution)/shard_map/all_gather | solution.py:105
  533.1 26.1 %convolution_convert_fusion.1 = bf16[1792,1024]{1,0:T(8,128)(2,1)} fusion(bf16[1024,1024]{0,1:T(8,128)(2,1)} %all-gather.9.cloned.1.call-done, bf16[1792,1024]{1,0:T(8,128)(2,1)} %add_convert_fusion.1, bf16[1024,1024]{1,0:T(8,128)(2,1)} %all-gather.7.cloned.1.call-done), kind=kOutput, calls=%fused_computation.84 | convolution fusion | flops 7637303296 | bytes 11534336 | tf_op jit(solution)/shard_map/dot_general | solution.py:128
  559.9 135.0 %all-gather.13.cloned.1.call-done = bf16[7168,1024]{1,0:T(8,128)(2,1)} async-done(((bf16[1792,1024]{1,0:T(8,128)(2,1)}), bf16[7168,1024]{1,0:T(8,128)(2,1)}) %all-gather.13.cloned.1.call-update) | async-done | bytes 14680080 | tf_op jit(solution)/shard_map/all_gather | solution.py:39
  694.9 11.3 %reduce_sum.122 = bf16[1792,1024]{1,0:T(8,128)(2,1)} reduce(bf16[4,1792,1024]{2,1,0:T(8,128)(2,1)} %bitcast.155, bf16[]{:T(256)} %constant.100.clone.1), dimensions={0}, to_apply=%region_24.25 | reduce | flops 5505024 | bytes 18350082 | tf_op jit(solution)/shard_map/reduce_sum | solution.py:39
  706.2 4.3 fusion.42
  710.5 5.0 multiply_reduce_fusion
  715.5 8.4 add_convert_fusion
  723.9 6.9 gather_fusion.2
  730.9 7.2 broadcast_select_fusion
  738.1 7.5 all-to-all-start.3
  745.7 1.4 pad_maximum_fusion
  747.0 3.6 copy.98
  750.6 100.9 %all-to-all-done.3 = bf16[32,128,1024]{2,1,0:T(8,128)(2,1)} async-done(((bf16[32,128,1024]{2,1,0:T(8,128)(2,1)}), bf16[32,128,1024]{2,1,0:T(8,128)(2,1)}, u32[]{:S(2)}, u32[]{:S(2)}) %all-to-all-start.3) | async-done | bytes 8388640 | tf_op jit(solution)/shard_map/all_to_all | solution.py:133
  851.5 6.0 gather_fusion.3
  (138 shorter events, 34.8 us)
Async XLA Ops:
  7.2 10.6 %copy-start = (s32[1792]{0:T(1024)S(1)}, s32[1792]{0:T(1024)}, u32[]{:S(2)}) copy-start(s32[1792]{0:T(1024)} %param.22) | copy-start | bytes 21508
  8.0 35.8 %copy-start.28 = (s32[14]{0:T(128)}, s32[14]{0:T(128)S(1)}, u32[]{:S(2)}) copy-start(s32[14]{0:T(128)S(1)} %compare_select_fusion.2) | copy-start | bytes 172
  9.3 15.8 %all-to-all-start = ((s32[32,1,1]{2,1,0:T(1,128)}), s32[32,1,1]{2,1,0:T(1,128)S(1)}, u32[]{:S(2)}, u32[]{:S(2)}) async-start(s32[32,1,1]{2,1,0:T(1,128)} %copy.81), calls=%async_computation | async-start | bytes 32768 | tf_op jit(solution)/shard_map/all_to_all | solution.py:91
  25.0 220.8 %copy-start.18 = (s32[32,1,1]{2,1,0:T(1,128)}, s32[32,1,1]{2,1,0:T(1,128)S(1)}, u32[]{:S(2)}) copy-start(s32[32,1,1]{2,1,0:T(1,128)S(1)} %all-to-all-done) | copy-start | bytes 388
  25.0 18.8 %all-to-all-start.2 = ((s32[32,1,128]{2,1,0:T(1,128)}), s32[32,1,128]{2,1,0:T(1,128)S(1)}, u32[]{:S(2)}, u32[]{:S(2)}) async-start(s32[32,1,128]{2,1,0:T(1,128)} %bitcast.17), calls=%async_computation.2 | async-start | bytes 32768 | tf_op jit(solution)/shard_map/all_to_all | solution.py:90
  43.8 7.8 copy-start.22
  43.8 127.1 %copy-start.23 = (bf16[32,256]{1,0:T(8,128)(2,1)S(1)}, bf16[32,256]{1,0:T(8,128)(2,1)}, u32[]{:S(2)}) copy-start(bf16[32,256]{1,0:T(8,128)(2,1)} %param.25) | copy-start | bytes 49156
  43.8 152.6 %copy-start.24 = (bf16[32,256]{1,0:T(8,128)(2,1)S(1)}, bf16[32,256]{1,0:T(8,128)(2,1)}, u32[]{:S(2)}) copy-start(bf16[32,256]{1,0:T(8,128)(2,1)} %param.26) | copy-start | bytes 49156
  43.8 174.7 %copy-start.25 = (bf16[256,32]{0,1:T(8,128)(2,1)S(1)}, bf16[256,32]{0,1:T(8,128)(2,1)}, u32[]{:S(2)}) copy-start(bf16[256,32]{0,1:T(8,128)(2,1)} %param.27) | copy-start | bytes 49156
  43.8 204.3 %all-to-all-start.1 = ((bf16[32,128,1024]{2,1,0:T(8,128)(2,1)}), bf16[32,128,1024]{2,1,0:T(8,128)(2,1)}, u32[]{:S(2)}, u32[]{:S(2)}) async-start(bf16[32,128,1024]{2,1,0:T(8,128)(2,1)} %scatter_fusion), calls=%async_computation.1 | async-start | bytes 16777216 | tf_op jit(solution)/shard_map/all_to_all | solution.py:89
  51.5 389.3 %all-gather.11.cloned.1.call-start = ((), (), s32[]{:S(2)}) async-start(), calls=%async_computation.6 | async-start | bytes 18350080 | tf_op jit(solution)/shard_map/all_gather | solution.py:39
  254.2 3.4 copy-start.2
  257.6 9.1 %copy-start.8 = (bf16[1792,256]{0,1:T(8,128)(2,1)}, bf16[1792,256]{0,1:T(8,128)(2,1)S(1)}, u32[]{:S(2)}) copy-start(bf16[1792,256]{0,1:T(8,128)(2,1)S(1)} %convolution_convert_fusion.2) | copy-start | bytes 2752516
  258.8 4.5 copy-start.10
  267.7 11.2 %copy-start.15 = (bf16[1792,64]{1,0:T(8,128)(2,1)S(1)}, bf16[1792,64]{1,0:T(8,128)(2,1)}, u32[]{:S(2)}) copy-start(bf16[1792,64]{1,0:T(8,128)(2,1)} %copy.102) | copy-start | bytes 688132
  267.7 11.2 %copy-start.16 = (bf16[1792,64]{1,0:T(8,128)(2,1)S(1)}, bf16[1792,64]{1,0:T(8,128)(2,1)}, u32[]{:S(2)}) copy-start(bf16[1792,64]{1,0:T(8,128)(2,1)} %copy.95) | copy-start | bytes 688132
  287.0 7.7 copy-start.11
  287.0 8.0 copy-start.13
  287.0 8.0 copy-start.14
  295.0 7.9 copy-start.12
  295.0 7.9 copy-start.17
  305.9 181.8 %all-gather.7.cloned.1.call-start = ((), (), s32[]{:S(2)}) async-start(), calls=%async_computation.4 | async-start | bytes 2162688 | tf_op jit(solution)/shard_map/all_gather | solution.py:103
  306.7 226.4 %all-gather.9.cloned.1.call-start = ((), (), s32[]{:S(2)}) async-start(), calls=%async_computation.5 | async-start | bytes 2162688 | tf_op jit(solution)/shard_map/all_gather | solution.py:105
  307.4 387.5 %all-gather.13.cloned.1.call-start = ((), (), s32[]{:S(2)}) async-start(), calls=%async_computation.7 | async-start | bytes 18350080 | tf_op jit(solution)/shard_map/all_gather | solution.py:39
  451.8 4.4 copy-start.3
  451.8 5.4 copy-start.5
  451.8 7.7 copy-start.20
  451.8 7.7 copy-start.21
  462.9 96.4 %copy-start.30 = (s32[32]{0:T(128)S(1)}, s32[32]{0:T(128)}, u32[]{:S(2)}) copy-start(s32[32]{0:T(128)} %get-tuple-element.304) | copy-start | bytes 388
  462.9 96.4 %copy-start.19 = (s32[32,1,1]{2,1,0:T(1,128)S(1)}, s32[32,1,1]{2,1,0:T(1,128)}, u32[]{:S(2)}) copy-start(s32[32,1,1]{2,1,0:T(1,128)} %copy-done.18) | copy-start | bytes 388
  706.2 9.3 %copy-start.4 = (bf16[14,128,1024]{2,1,0:T(8,128)(2,1)S(1)}, bf16[14,128,1024]{2,1,0:T(8,128)(2,1)}, u32[]{:S(2)}) copy-start(bf16[14,128,1024]{2,1,0:T(8,128)(2,1)} %gather_fusion) | copy-start | bytes 11010052
  706.2 9.3 %copy-start.6 = (bf16[1792,1024]{1,0:T(8,128)(2,1)S(1)}, bf16[1792,1024]{1,0:T(8,128)(2,1)}, u32[]{:S(2)}) copy-start(bf16[1792,1024]{1,0:T(8,128)(2,1)} %reduce_sum.119) | copy-start | bytes 11010052
  706.2 9.3 %copy-start.7 = (bf16[1792,1024]{1,0:T(8,128)(2,1)S(1)}, bf16[1792,1024]{1,0:T(8,128)(2,1)}, u32[]{:S(2)}) copy-start(bf16[1792,1024]{1,0:T(8,128)(2,1)} %reduce_sum.122) | copy-start | bytes 11010052
  706.2 9.3 %copy-start.26 = (f32[1024]{0:T(1024)S(1)}, f32[1024]{0:T(1024)}, u32[]{:S(2)}) copy-start(f32[1024]{0:T(1024)} %param.33) | copy-start | bytes 12292
  706.2 9.4 %copy-start.27 = (f32[1024]{0:T(1024)S(1)}, f32[1024]{0:T(1024)}, u32[]{:S(2)}) copy-start(f32[1024]{0:T(1024)} %param.32) | copy-start | bytes 12292
  738.1 7.5 copy-start.29
  738.1 7.6 copy-start.9
  738.1 113.4 %all-to-all-start.3 = ((bf16[32,128,1024]{2,1,0:T(8,128)(2,1)}), bf16[32,128,1024]{2,1,0:T(8,128)(2,1)}, u32[]{:S(2)}, u32[]{:S(2)}) async-start(bf16[32,128,1024]{2,1,0:T(8,128)(2,1)} %broadcast_select_fusion), calls=%async_computation.3 | async-start | bytes 16777216 | tf_op jit(solution)/shard_map/all_to_all | solution.py:133
  745.7 111.9 %copy-start.1 = (s32[1792]{0:T(1024)S(1)}, s32[1792]{0:T(1024)}, u32[]{:S(2)}) copy-start(s32[1792]{0:T(1024)} %param.22) | copy-start | bytes 21508
Sparse Core Ops, SparseCore 0:
  306.1 134.6 all-gather.10
  443.0 44.7 all-gather.6
  490.0 42.9 all-gather.8
  559.4 135.4 all-gather.12
